TPU v7x, 256 devices: a whole 4x4x8 slice. The times are simulated.
256 devices in a mesh: ctx: 8 (over x, core), ch: 32 (over y, z).
Axes of the slice: x: 4, y: 4, z: 8, core: 2. Of those that a mesh axis runs over, the one named last changes fastest.
Arguments:
- tokens_in: bfloat16 [8192, 8192], P(('ctx', 'ch')), may hold values from -6 to 6
- norm_gain: float32 [8192], replicated, may hold values from 0.1 to 1.9
- proj_weight: bfloat16 [3, 8192, 8192], P(None, 'ctx', 'ch'), may hold values from -0.0625 to 0.0625
- conv_weight: float32 [3, 7, 8192], P(None, None, 'ch'), may hold values from -2 to 2
- decay_rate: float32 [16, 8192], P(None, 'ch'), may hold values from 6.1035157e-06 to 0.04
- residue: float32 [16, 8192], P(None, 'ch'), may hold values from -1.5 to 1.5
- skip_gain: float32 [8192], P('ch'), may hold values from -3 to 3
Outputs:
- gated: bfloat16 [8192, 8192], P(('ctx', 'ch'))
All inputs are finite; a program needn't handle non-finite values.
Results may differ from a plain program's by a relative error of at most 0.008.
Values may be sent and summed in bfloat16 or wider, within the bound.
No kernel may reach another device: no remote copies, remote signals or barrier semaphores. Data moves between devices by JAX's collectives and lax.ppermute only.
A program may use at most 128 MiB of HBM per device.

v0:
```python
import jax
import jax.numpy as jnp
from jax import lax
from jax.sharding import PartitionSpec as P

norm_eps = 1e-05


def shifted(shard, axis, by):
    length = lax.axis_size(axis)
    pairs = [(i, i + by) for i in range(length) if 0 <= i + by < length]
    return lax.ppermute(shard, axis, pairs)


def on_device(tokens_in, norm_gain, proj_weight, conv_weight, decay_rate, residue, skip_gain):
    widened = tokens_in.astype(jnp.float32)
    mean_square = jnp.mean(widened * widened, axis=-1, keepdims=True)
    normed = (widened * lax.rsqrt(mean_square + norm_eps) * norm_gain[None, :]).astype(jnp.bfloat16)
    gathered = lax.all_gather(normed, "ch", axis=0, tiled=True)
    row_count = gathered.shape[0]
    chan_count = proj_weight.shape[2]
    summed = jnp.einsum(
        "tf,ifc->itc",
        gathered,
        lax.all_gather(proj_weight, "ctx", axis=1, tiled=True),
        preferred_element_type=jnp.float32,
    )
    projected = summed.astype(jnp.bfloat16)
    tap_count = conv_weight.shape[1]
    reach = tap_count - 1
    rim_rows = shifted(projected[:, row_count - reach :, :], "ctx", 1)
    padded = jnp.concatenate([rim_rows, projected], axis=1).astype(jnp.float32)
    featured = jnp.zeros((3, row_count, chan_count), jnp.float32)
    for shift_idx in range(tap_count):
        featured = (
            featured
            + conv_weight[:, shift_idx, None, :]
            * padded[:, reach - shift_idx : reach - shift_idx + row_count, :]
        )
    queries = featured[0]
    mixed = featured[1] * featured[2]
    highest = lax.Precision.HIGHEST
    in_scale = jnp.sqrt(-jnp.expm1(-2.0 * decay_rate))
    span_rows = min(128, row_count)
    span_count = row_count // span_rows
    positions = jnp.arange(span_rows, dtype=jnp.float32)
    lag_decay = jnp.exp(-decay_rate[:, None, :] * positions[None, :, None])
    impulse = jnp.sum((residue * in_scale)[:, None, :] * lag_decay, axis=0)
    offsets = jnp.arange(span_rows)[:, None] - jnp.arange(span_rows)[None, :]
    lag_table = (offsets[None, :, :] == jnp.arange(span_rows)[:, None, None]).astype(jnp.float32)
    toeplitz = jnp.einsum("lc,lts->cts", impulse, lag_table, precision=highest)
    spans_in = mixed.reshape(span_count, span_rows, chan_count)
    inside = jnp.einsum("cts,jsc->jtc", toeplitz, spans_in, precision=highest)
    end_weight = in_scale[:, None, :] * jnp.exp(
        -decay_rate[:, None, :] * (span_rows - 1.0 - positions)[None, :, None]
    )
    span_ends = jnp.einsum("jsc,msc->jmc", spans_in, end_weight, precision=highest)
    span_decay = jnp.exp(-decay_rate * float(span_rows))

    def advance(carried, span_end):
        return (span_decay * carried + span_end, carried)

    zero_state = jnp.zeros(decay_rate.shape, jnp.float32)
    local_end, starts = lax.scan(advance, zero_state, span_ends)
    whole_decay = jnp.exp(-decay_rate * float(row_count))

    def handoff(unused_turn, incoming):
        return shifted(whole_decay * incoming + local_end, "ctx", 1)

    incoming = lax.fori_loop(0, lax.axis_size("ctx") - 1, handoff, zero_state)
    span_starts = jnp.arange(span_count, dtype=jnp.float32) * float(span_rows)
    starts = (
        starts
        + jnp.exp(-decay_rate[None, :, :] * span_starts[:, None, None]) * incoming[None, :, :]
    )
    out_weight = residue[:, None, :] * jnp.exp(
        -decay_rate[:, None, :] * (positions + 1.0)[None, :, None]
    )
    outside = jnp.einsum("jmc,mtc->jtc", starts, out_weight, precision=highest)
    filtered = (inside + outside).reshape(row_count, chan_count)
    gated = (queries * (filtered + skip_gain[None, :] * mixed)).astype(jnp.bfloat16)
    return lax.all_to_all(gated, "ch", split_axis=0, concat_axis=1, tiled=True)


def solution(mesh):
    in_specs = (
        P(("ctx", "ch"), None),
        P(),
        P(None, "ctx", "ch"),
        P(None, None, "ch"),
        P(None, "ch"),
        P(None, "ch"),
        P("ch"),
    )
    out_specs = P(("ctx", "ch"), None)
    return jax.shard_map(
        on_device, mesh=mesh, in_specs=in_specs, out_specs=out_specs, check_vma=False
    )
```

profile of v0, /device:TPU:34, one launch (start us, length us, event | category | flops | bytes accessed | tf_op | source)
XLA Modules:
  0.0 376.8 jit_solution(1986812862186608656)
XLA Ops:
  6.5 0.7 all-gather.5.cloned.1.call-update
  7.3 1.3 fusion.38
  8.6 2.0 fusion.40
  10.9 1.7 multiply_reduce_fusion
  12.7 9.6 %fusion.4 = f32[256,128,128]{2,0,1:T(8,128)} fusion(s32[128,128]{1,0:T(8,128)S(1)} %iota_subtract_fusion, f32[128,256]{0,1:T(8,128)S(1)} %multiply_reduce_fusion), kind=kOutput, calls=%fused_computation.8 | convolution fusion | flops 6444548096 | bytes 16973824 | tf_op jit(solution)/shard_map/lc,lts->cts/dot_general | solution.py:51
  22.2 58.8 %all-gather.5.cloned.1.call-done = bf16[3,8192,256]{2,1,0:T(8,128)(2,1)} async-done(((bf16[3,1024,256]{2,1,0:T(8,128)(2,1)}), bf16[3,8192,256]{2,1,0:T(8,128)(2,1)}) %all-gather.5.cloned.1.call-update) | async-done | bytes 12582928 | tf_op jit(solution)/shard_map/all_gather | solution.py:25
  81.0 141.5 %all-gather.3.cloned.1.call-done = bf16[1024,8192]{1,0:T(8,128)(2,1)} async-done(((bf16[32,8192]{1,0:T(8,128)(2,1)}), bf16[1024,8192]{1,0:T(8,128)(2,1)}) %all-gather.3.cloned.1.call-update) | async-done | bytes 16777232 | tf_op jit(solution)/shard_map/all_gather | solution.py:19
  222.6 18.7 %fusion.23 = bf16[3,1024,256]{2,1,0:T(8,128)(2,1)S(1)} fusion(bf16[3,8192,256]{2,1,0:T(8,128)(2,1)} %all-gather.5.cloned.1.call-done, bf16[1024,8192]{1,0:T(8,128)(2,1)} %all-gather.3.cloned.1.call-done), kind=kOutput, calls=%fused_computation.34 | convolution fusion | flops 12885688320 | bytes 30932992 | tf_op jit(solution)/shard_map/tf,ifc->itc/dot_general | solution.py:22
  241.3 2.1 collective-permute-start.1
  243.4 0.7 copy.31
  244.3 2.0 collective-permute-done.1
  246.3 0.3 maximum_convert_fusion
  246.6 2.6 fusion.6
  249.4 0.4 copy.29
  249.8 38.4 %fusion.32 = f32[8,128,256]{1,0,2:T(8,128)} fusion(f32[8,128,256]{1,0,2:T(8,128)S(1)} %copy.29, f32[256,128,128]{2,0,1:T(8,128)} %fusion.4), kind=kOutput, calls=%fused_computation.37 | convolution fusion | flops 402653184 | bytes 18874368 | tf_op jit(solution)/shard_map/cts,jsc->jtc/dot_general | solution.py:53
  288.2 5.2 %fusion.29 = f32[8,16,256]{1,0,2:T(8,128)} fusion(f32[8,128,256]{1,0,2:T(8,128)S(1)} %copy.29, f32[128]{0:T(128)S(1)} %iota_subtract_fusion.1, f32[16,256]{0,1:T(8,128)S(1)} %copy.32, f32[16,256]{0,1:T(8,128)S(1)} %copy.28), kind=kOutput, calls=%fused_computation.36 | convolution fusion | flops 51380224 | bytes 1212928 | tf_op jit(solution)/shard_map/jsc,msc->jmc/dot_general | solution.py:57
  293.4 1.6 copy.34
  295.0 4.9 %while.24 = (s32[]{:T(128)}, f32[16,256]{1,0:T(8,128)S(1)}, f32[8,16,256]{2,1,0:T(8,128)}, f32[16,256]{1,0:T(8,128)S(1)}, f32[8,16,256]{2,1,0:T(8,128)S(1)}, /*index=5*/s32[]{:T(128)}, s32[]{:T(128)}) while((s32[]{:T(128)}, f32[16,256]{1,0:T(8,128)S(1)}, f32[8,16,256]{2,1,0:T(8,128)}, f32[16,256]{1,0:T(8,128)S(1)}, ...), condition=%wide.region_3.4_spmd.clone, body=%wide.region_2.3_spmd.clone.sunk | while | flops 16387 | bytes 98408 | solution.py:64
  295.0 0.6 bitcast_dynamic-update-slice_fusion.2
  295.6 0.6 bitcast_dynamic-update-slice_fusion.2
  296.2 0.6 bitcast_dynamic-update-slice_fusion.2
  296.8 0.6 bitcast_dynamic-update-slice_fusion.2
  297.4 0.6 bitcast_dynamic-update-slice_fusion.2
  298.1 0.6 bitcast_dynamic-update-slice_fusion.2
  298.7 0.6 bitcast_dynamic-update-slice_fusion.2
  299.3 0.6 bitcast_dynamic-update-slice_fusion.2
  299.9 35.4 %while.23 = (s32[]{:T(128)}, f32[16,256]{1,0:T(8,128)S(1)}, f32[16,256]{1,0:T(8,128)S(1)}, f32[16,256]{1,0:T(8,128)S(1)}, s32[]{:T(128)}) while((s32[]{:T(128)}, f32[16,256]{1,0:T(8,128)S(1)}, f32[16,256]{1,0:T(8,128)S(1)}, f32[16,256]{1,0:T(8,128)S(1)}, s32[]{:T(128)}) %tuple.55), condition=%wide.region_5.6_spmd, body=%wide.region_4.5_spmd.sunk | while | flops 8194 | bytes 131173 | solution.py:70
  299.9 1.9 collective-permute-start
  301.9 3.1 collective-permute-done
  305.0 1.9 collective-permute-start
  306.9 3.1 collective-permute-done
  310.1 1.9 collective-permute-start
  312.0 3.1 collective-permute-done
  315.1 1.9 collective-permute-start
  317.0 3.1 collective-permute-done
  320.2 1.9 collective-permute-start
  322.1 3.1 collective-permute-done
  325.2 1.9 collective-permute-start
  327.1 3.1 collective-permute-done
  330.3 1.9 collective-permute-start
  332.2 3.1 collective-permute-done
  335.3 1.0 multiply_add_fusion.1
  336.3 1.3 copy.35
  337.7 5.0 %fusion.35 = f32[8,128,256]{1,0,2:T(8,128)} fusion(f32[8,128,256]{1,0,2:T(8,128)S(1)} %copy-done, f32[8,16,256]{1,0,2:T(8,128)} %copy.35, f32[128]{0:T(128)S(1)} %iota_add_fusion, f32[16,256]{0,1:T(8,128)} %copy.31, f32[16,256]{0,1:T(8,128)S(1)} %copy.28), kind=kOutput, calls=%fused_computation.38 | convolution fusion | flops 51642368 | bytes 2261504 | tf_op jit(solution)/shard_map/jmc,mtc->jtc/dot_general | solution.py:79
  342.6 1.6 copy.36
  344.2 0.4 multiply_convert_fusion
  344.6 24.5 %all_to_all.16 = bf16[32,32,256]{2,1,0:T(8,128)(2,1)S(1)} all-to-all(bf16[32,32,256]{2,1,0:T(8,128)(2,1)S(1)} %multiply_convert_fusion), channel_id=1, replica_groups=mesh['ctx'=8,'ch'=32] {'ch'}, dimensions={0} | all-to-all | bytes 1048576 | tf_op jit(solution)/shard_map/all_to_all | solution.py:82
  369.1 0.8 copy.45
  (47 shorter events, 0.8 us)
Async XLA Ops:
  6.5 4.1 %copy-start.3 = (f32[16,256]{1,0:T(8,128)S(1)}, f32[16,256]{1,0:T(8,128)}, u32[]{:S(2)}) copy-start(f32[16,256]{1,0:T(8,128)} %param.15) | copy-start | bytes 49156
  6.5 4.1 %copy-start.1 = (f32[16,256]{1,0:T(8,128)S(1)}, f32[16,256]{1,0:T(8,128)}, u32[]{:S(2)}) copy-start(f32[16,256]{1,0:T(8,128)} %param.16) | copy-start | bytes 49156
  6.5 6.1 %copy-start.2 = (f32[3,7,256]{2,1,0:T(8,128)S(1)}, f32[3,7,256]{2,1,0:T(8,128)}, u32[]{:S(2)}) copy-start(f32[3,7,256]{2,1,0:T(8,128)} %param.14) | copy-start | bytes 64516
  6.5 74.5 %all-gather.5.cloned.1.call-start = ((), (), s32[]{:S(2)}) async-start(), calls=%async_computation.2 | async-start | bytes 14155776 | tf_op jit(solution)/shard_map/all_gather | solution.py:25
  7.3 215.3 %all-gather.3.cloned.1.call-start = ((), (), s32[]{:S(2)}) async-start(), calls=%async_computation.1 | async-start | bytes 17301504 | tf_op jit(solution)/shard_map/all_gather | solution.py:19
  241.3 5.0 %collective-permute-start.1 = (bf16[3,6,256]{2,1,0:T(8,128)(2,1)S(1)}, bf16[3,6,256]{2,1,0:T(8,128)(2,1)S(1)}, u32[]{:S(2)}, u32[]{:S(2)}) collective-permute-start(bf16[3,6,256]{2,1,0:T(8,128)(2,1)S(1)} %slice.72), channel_id=1, source_target_pairs={{0,32},{32,64},{64,96},{96,128},{128,160},{160,192},{192,224},{1,3... | collective-permute-start | bytes 27656 | tf_op jit(solution)/shard_map/ppermute | solution.py:12
  293.4 44.3 %copy-start = (f32[8,128,256]{1,0,2:T(8,128)S(1)}, f32[8,128,256]{1,0,2:T(8,128)}, u32[]{:S(2)}) copy-start(f32[8,128,256]{1,0,2:T(8,128)} %fusion.32) | copy-start | bytes 3145732
  299.9 5.1 %collective-permute-start = (f32[16,256]{1,0:T(8,128)S(1)}, f32[16,256]{1,0:T(8,128)S(1)}, u32[]{:S(2)}, u32[]{:S(2)}) collective-permute-start(f32[16,256]{1,0:T(8,128)S(1)} %multiply_add_fusion.3), channel_id=1, source_target_pairs={{0,32},{32,64},{64,96},{96,128},{128,160},{160,192},{192,224},{1,3... | collective-permute-start | bytes 49160 | tf_op jit(solution)/shard_map/while/body/eval_jaxpr/ppermute | solution.py:12
  305.0 5.0 %collective-permute-start = (f32[16,256]{1,0:T(8,128)S(1)}, f32[16,256]{1,0:T(8,128)S(1)}, u32[]{:S(2)}, u32[]{:S(2)}) collective-permute-start(f32[16,256]{1,0:T(8,128)S(1)} %multiply_add_fusion.3), channel_id=1, source_target_pairs={{0,32},{32,64},{64,96},{96,128},{128,160},{160,192},{192,224},{1,3... | collective-permute-start | bytes 49160 | tf_op jit(solution)/shard_map/while/body/eval_jaxpr/ppermute | solution.py:12
  310.1 5.0 %collective-permute-start = (f32[16,256]{1,0:T(8,128)S(1)}, f32[16,256]{1,0:T(8,128)S(1)}, u32[]{:S(2)}, u32[]{:S(2)}) collective-permute-start(f32[16,256]{1,0:T(8,128)S(1)} %multiply_add_fusion.3), channel_id=1, source_target_pairs={{0,32},{32,64},{64,96},{96,128},{128,160},{160,192},{192,224},{1,3... | collective-permute-start | bytes 49160 | tf_op jit(solution)/shard_map/while/body/eval_jaxpr/ppermute | solution.py:12
  315.1 5.0 %collective-permute-start = (f32[16,256]{1,0:T(8,128)S(1)}, f32[16,256]{1,0:T(8,128)S(1)}, u32[]{:S(2)}, u32[]{:S(2)}) collective-permute-start(f32[16,256]{1,0:T(8,128)S(1)} %multiply_add_fusion.3), channel_id=1, source_target_pairs={{0,32},{32,64},{64,96},{96,128},{128,160},{160,192},{192,224},{1,3... | collective-permute-start | bytes 49160 | tf_op jit(solution)/shard_map/while/body/eval_jaxpr/ppermute | solution.py:12
  320.2 5.0 %collective-permute-start = (f32[16,256]{1,0:T(8,128)S(1)}, f32[16,256]{1,0:T(8,128)S(1)}, u32[]{:S(2)}, u32[]{:S(2)}) collective-permute-start(f32[16,256]{1,0:T(8,128)S(1)} %multiply_add_fusion.3), channel_id=1, source_target_pairs={{0,32},{32,64},{64,96},{96,128},{128,160},{160,192},{192,224},{1,3... | collective-permute-start | bytes 49160 | tf_op jit(solution)/shard_map/while/body/eval_jaxpr/ppermute | solution.py:12
  325.2 5.0 %collective-permute-start = (f32[16,256]{1,0:T(8,128)S(1)}, f32[16,256]{1,0:T(8,128)S(1)}, u32[]{:S(2)}, u32[]{:S(2)}) collective-permute-start(f32[16,256]{1,0:T(8,128)S(1)} %multiply_add_fusion.3), channel_id=1, source_target_pairs={{0,32},{32,64},{64,96},{96,128},{128,160},{160,192},{192,224},{1,3... | collective-permute-start | bytes 49160 | tf_op jit(solution)/shard_map/while/body/eval_jaxpr/ppermute | solution.py:12
  330.3 5.0 %collective-permute-start = (f32[16,256]{1,0:T(8,128)S(1)}, f32[16,256]{1,0:T(8,128)S(1)}, u32[]{:S(2)}, u32[]{:S(2)}) collective-permute-start(f32[16,256]{1,0:T(8,128)S(1)} %multiply_add_fusion.3), channel_id=1, source_target_pairs={{0,32},{32,64},{64,96},{96,128},{128,160},{160,192},{192,224},{1,3... | collective-permute-start | bytes 49160 | tf_op jit(solution)/shard_map/while/body/eval_jaxpr/ppermute | solution.py:12
  337.7 6.5 %copy-start.4 = (f32[256]{0:T(256)S(1)}, f32[256]{0:T(256)}, u32[]{:S(2)}) copy-start(f32[256]{0:T(256)} %param.17) | copy-start | bytes 3076
Sparse Core Ops, SparseCore 0:
  9.2 71.7 all-gather.4
  83.6 138.9 all-gather.2
where the time goes:
time: 377 us
  waiting for transfers between devices  225 us (60%)
  matrix products  76.7 us (20%)
  blocking collectives  24.5 us (6%)
  starting transfers between devices  15.5 us (4%)
  other arithmetic  14.5 us (4%)
  between operations  13.6 us (4%)
  local copies, waits for them, and re-layouts  6.84 us (2%)
    all_gather x1, waiting for transfers between devices, on_device(): gathered = lax.all_gather(normed, 'ch', axis=0, tiled=True)  142 us
    all_gather x1, waiting for transfers between devices, on_device(): lax.all_gather(proj_weight, 'ctx', axis=1, tiled=True)  58.8 us
    dot_general x1, matrix products, on_device(): inside = jnp.einsum('cts,jsc->jtc', toeplitz, spans_in, precision=highest)  38.4 us
    all_to_all x1, blocking collectives, on_device(): return lax.all_to_all(gated, 'ch', split_axis=0, concat_axis=1, tiled=True)  24.5 us
    ppermute x8, waiting for transfers between devices, shifted(): return lax.ppermute(shard, axis, pairs)  23.9 us
    dot_general x1, matrix products, on_device(): jnp.einsum('tf,ifc->itc', gathered, lax.all_gather(proj_weight, 'ctx', ax...  18.7 us
    ppermute x8, starting transfers between devices, shifted(): return lax.ppermute(shard, axis, pairs)  15.5 us
    dot_general x1, matrix products, on_device(): toeplitz = jnp.einsum('lc,lts->cts', impulse, lag_table, precision=highest)  9.55 us
  transfers between devices with their start and end apart: 10, of which 10 were waited for; matrix products, arithmetic and copies ran while one was open for 4% of the time, Pallas kernels for 0%

commit v1 on v0

--- a/solution.py
+++ b/solution.py
@@ -19,11 +19,39 @@
     gathered = lax.all_gather(normed, "ch", axis=0, tiled=True)
     row_count = gathered.shape[0]
     chan_count = proj_weight.shape[2]
-    summed = jnp.einsum(
-        "tf,ifc->itc",
-        gathered,
-        lax.all_gather(proj_weight, "ctx", axis=1, tiled=True),
-        preferred_element_type=jnp.float32,
+
+    def extend_notes_all(target, link_axis, local):
+        block_list = []
+        local_out, step_out, tall = (
+            lax.axis_size(link_axis),
+            lax.axis_index(link_axis),
+            target.shape[1],
+        )
+        for d in [*range(local_out)]:
+            block_list.append((d, (d + 1) % local_out))
+        copies = []
+        for d in [*range(local_out)]:
+            copies.append((d, (d - 1) % local_out))
+        now = local_out // 2
+        z2 = v_next = target
+        lower = local(target, step_out * tall)
+        for at in tuple(range(1, now + 1)):
+            z2 = lax.ppermute(z2, perm=block_list, axis_name=link_axis)
+            if at < local_out - now:
+                v_next = lax.ppermute(v_next, axis_name=link_axis, perm=copies)
+                lower = lower + local(v_next, (step_out + at) % local_out * tall)
+            lower = lower + local(z2, (step_out - at) % local_out * tall)
+        return lower
+
+    summed = extend_notes_all(
+        proj_weight,
+        "ctx",
+        local=lambda part, offset: jnp.einsum(
+            "tf,ifc->itc",
+            lax.dynamic_slice_in_dim(gathered, offset, part.shape[1], axis=1),
+            part,
+            preferred_element_type=jnp.float32,
+        ),
     )
     projected = summed.astype(jnp.bfloat16)
     tap_count = conv_weight.shape[1]

time: 377 us -> 313 us (0.83)
  waiting for transfers between devices: 225 us -> 147 us
  matrix products: 76.7 us -> 83.8 us
  starting transfers between devices: 15.5 us -> 20.4 us
    all_gather x1, waiting for transfers between devices: 142 us -> 80.5 us  [on_device(): gathered = lax.all_gather(normed, 'ch', axis=0, tiled=True)]
    all_gather x1 -> x0, waiting for transfers between devices: 58.8 us -> none  [on_device(): lax.all_gather(proj_weight, 'ctx', axis=1, tiled=True)]
    ppermute x0 -> x7, waiting for transfers between devices: none -> 42.6 us  [the longest x4 42.6 us: extend_notes_all(): z2 = lax.ppermute(z2, perm=block_list, axis_name=link_axis)]
    dot_general x1 -> x8, matrix products: 18.7 us -> 27.5 us  [on_device(): jnp.einsum('tf,ifc->itc', lax.dynamic_slice_in_dim(gathered, offset, part...]
    ppermute x0 -> x7, starting transfers between devices: none -> 5.06 us  [the longest x3 5.03 us: extend_notes_all(): v_next = lax.ppermute(v_next, axis_name=link_axis, perm=copies)]
  transfers between devices with their start and end apart: 10 -> 16, of which waited for: 10 -> 12; matrix products, arithmetic and copies ran while one was open for 4% -> 11% of each run, Pallas kernels for 0% -> 0%
where the time goes in v1:
time: 313 us; the launch traced here: 312 us
  waiting for transfers between devices  147 us (47%)
  matrix products  83.8 us (27%)
  blocking collectives  24.5 us (8%)
  starting transfers between devices  20.4 us (7%)
  other arithmetic  15.5 us (5%)
  between operations  13.8 us (4%)
  local copies, waits for them, and re-layouts  6.79 us (2%)
    all_gather x1, waiting for transfers between devices, on_device(): gathered = lax.all_gather(normed, 'ch', axis=0, tiled=True)  80.5 us
    ppermute x4, waiting for transfers between devices, extend_notes_all(): z2 = lax.ppermute(z2, perm=block_list, axis_name=link_axis)  42.6 us
    dot_general x1, matrix products, on_device(): inside = jnp.einsum('cts,jsc->jtc', toeplitz, spans_in, precision=highest)  37.7 us
    dot_general x8, matrix products, on_device(): jnp.einsum('tf,ifc->itc', lax.dynamic_slice_in_dim(gathered, offset, part...  27.5 us
    all_to_all x1, blocking collectives, on_device(): return lax.all_to_all(gated, 'ch', split_axis=0, concat_axis=1, tiled=True)  24.5 us
    ppermute x8, waiting for transfers between devices, shifted(): return lax.ppermute(shard, axis, pairs)  24.1 us
    ppermute x8, starting transfers between devices, shifted(): return lax.ppermute(shard, axis, pairs)  15.3 us
    dot_general x1, matrix products, on_device(): toeplitz = jnp.einsum('lc,lts->cts', impulse, lag_table, precision=highest)  9.55 us
  transfers between devices with their start and end apart: 16, of which 12 were waited for; matrix products, arithmetic and copies ran while one was open for 11% of the time, Pallas kernels for 0%

profile of v1, /device:TPU:34, one launch (start us, length us, event | category | flops | bytes accessed | tf_op | source)
XLA Modules:
  0.0 312.0 jit_solution(15841955197676510585)
XLA Ops:
  6.5 1.3 fusion.57
  7.8 2.0 fusion.59
  9.9 1.7 collective-permute-start.1
  11.6 18.3 %collective-permute-done.2 = bf16[3,1024,256]{2,1,0:T(8,128)(2,1)S(1)} collective-permute-done((bf16[3,1024,256]{2,1,0:T(8,128)(2,1)}, bf16[3,1024,256]{2,1,0:T(8,128)(2,1)S(1)}, u32[]{:S(2)}, u32[]{:S(2)}) %collective-permute-start.2) | collective-permute-done | bytes 1572896 | tf_op jit(solution)/shard_map/ppermute | solution.py:39
  29.9 0.8 multiply_exponential_fusion
  31.0 1.7 multiply_reduce_fusion
  32.7 1.7 collective-permute-start.3
  34.4 15.5 %collective-permute-done.4 = bf16[3,1024,256]{2,1,0:T(8,128)(2,1)} collective-permute-done((bf16[3,1024,256]{2,1,0:T(8,128)(2,1)S(1)}, bf16[3,1024,256]{2,1,0:T(8,128)(2,1)}, u32[]{:S(2)}, u32[]{:S(2)}) %collective-permute-start.4) | collective-permute-done | bytes 1572896 | tf_op jit(solution)/shard_map/ppermute | solution.py:39
  50.1 9.5 %fusion.2 = f32[256,128,128]{2,0,1:T(8,128)} fusion(s32[128,128]{1,0:T(8,128)S(1)} %iota_subtract_fusion, f32[128,256]{0,1:T(8,128)S(1)} %multiply_reduce_fusion), kind=kOutput, calls=%fused_computation.6 | convolution fusion | flops 6444548096 | bytes 16973824 | tf_op jit(solution)/shard_map/lc,lts->cts/dot_general | solution.py:79
  59.7 1.6 collective-permute-start.5
  61.2 8.8 %collective-permute-done.6 = bf16[3,1024,256]{2,1,0:T(8,128)(2,1)} collective-permute-done((bf16[3,1024,256]{2,1,0:T(8,128)(2,1)}, bf16[3,1024,256]{2,1,0:T(8,128)(2,1)}, u32[]{:S(2)}, u32[]{:S(2)}) %collective-permute-start.6) | collective-permute-done | bytes 1572896 | tf_op jit(solution)/shard_map/ppermute | solution.py:39
  70.0 80.5 %all-gather.2.cloned.1.call-done = bf16[1024,8192]{1,0:T(8,128)(2,1)} async-done(((bf16[32,8192]{1,0:T(8,128)(2,1)}), bf16[1024,8192]{1,0:T(8,128)(2,1)}) %all-gather.2.cloned.1.call-update) | async-done | bytes 16777232 | tf_op jit(solution)/shard_map/all_gather | solution.py:19
  150.5 4.0 %fusion.12 = f32[1024,3,256]{2,0,1:T(8,128)S(1)} fusion(bf16[3,1024,256]{2,1,0:T(8,128)(2,1)} %collective-permute-done.6, bf16[1024,8192]{1,0:T(8,128)(2,1)} %all-gather.2.cloned.1.call-done, s32[]{:T(128)S(6)} %select_n.67), kind=kOutput, calls=%fused_computation.24 | convolution fusion | flops 1610612736 | bytes 6815748 | tf_op jit(solution)/shard_map/tf,ifc->itc/dot_general | solution.py:49
  154.5 4.6 %fusion.16 = f32[1024,3,256]{2,0,1:T(8,128)S(1)} fusion(bf16[3,1024,256]{2,1,0:T(8,128)(2,1)} %collective-permute-done.4, bf16[1024,8192]{1,0:T(8,128)(2,1)} %all-gather.2.cloned.1.call-done, s32[]{:T(128)S(6)} %select_n.63), kind=kOutput, calls=%fused_computation.28 | convolution fusion | flops 1610612736 | bytes 6815748 | tf_op jit(solution)/shard_map/tf,ifc->itc/dot_general | solution.py:49
  159.1 3.3 %fusion.18 = f32[1024,3,256]{2,0,1:T(8,128)S(1)} fusion(bf16[3,1024,256]{2,1,0:T(8,128)(2,1)} %collective-permute-done.3, bf16[1024,8192]{1,0:T(8,128)(2,1)S(1)} %copy-done.1, s32[]{:T(128)S(6)} %select_n.61), kind=kOutput, calls=%fused_computation.30 | convolution fusion | flops 1610612736 | bytes 6815748 | tf_op jit(solution)/shard_map/tf,ifc->itc/dot_general | solution.py:49
  162.5 1.8 fusion.20
  164.3 3.3 %fusion.22 = f32[1024,3,256]{2,0,1:T(8,128)S(1)} fusion(bf16[3,1024,256]{2,1,0:T(8,128)(2,1)} %collective-permute-done.1, bf16[1024,8192]{1,0:T(8,128)(2,1)S(1)} %copy-done.1, s32[]{:T(128)S(6)} %select_n.57), kind=kOutput, calls=%fused_computation.34 | convolution fusion | flops 1610612736 | bytes 6815748 | tf_op jit(solution)/shard_map/tf,ifc->itc/dot_general | solution.py:49
  167.6 1.8 fusion.24
  169.5 3.4 %fusion.14 = f32[1024,3,256]{2,0,1:T(8,128)} fusion(bf16[3,1024,256]{2,1,0:T(8,128)(2,1)S(1)} %collective-permute-done.5, bf16[1024,8192]{1,0:T(8,128)(2,1)S(1)} %copy-done.1, s32[]{:T(128)S(6)} %select_n.65), kind=kOutput, calls=%fused_computation.26 | convolution fusion | flops 1610612736 | bytes 6815748 | tf_op jit(solution)/shard_map/tf,ifc->itc/dot_general | solution.py:49
  172.9 5.2 %fusion.42 = bf16[3,1024,256]{2,1,0:T(8,128)(2,1)S(1)} fusion(f32[1024,3,256]{2,0,1:T(8,128)S(1)} %fusion.12, f32[1024,3,256]{2,0,1:T(8,128)} %fusion.14, f32[1024,3,256]{2,0,1:T(8,128)S(1)} %fusion.16, f32[1024,3,256]{2,0,1:T(8,128)S(1)} %fusion.18, f32[1024,3,256]{2,0,1:T(8,128)S(1)} %fusion.20, f32[1024,3,256]{2,0,1:T(8,128)S(1)} %fusion.24, ...), kind=kOutput, calls=%fused_computation.56 | convolution fusion | flops 1616904192 | bytes 27262980 | tf_op jit(solution)/shard_map/tf,ifc->itc/dot_general | solution.py:49
  178.2 1.9 collective-permute-start.8
  181.0 2.2 collective-permute-done.8
  183.5 2.8 fusion.4
  186.9 5.2 %fusion.46 = f32[8,16,256]{1,0,2:T(8,128)} fusion(f32[8,128,256]{1,0,2:T(8,128)S(1)} %copy.29, f32[128]{0:T(128)S(1)} %iota_subtract_fusion.1, f32[16,256]{0,1:T(8,128)S(1)} %copy.32, f32[16,256]{0,1:T(8,128)S(1)} %copy.28), kind=kOutput, calls=%fused_computation.58 | convolution fusion | flops 51380224 | bytes 1212928 | tf_op jit(solution)/shard_map/jsc,msc->jmc/dot_general | solution.py:85
  192.1 1.5 copy.34
  193.6 4.9 %while.24 = (s32[]{:T(128)}, f32[16,256]{1,0:T(8,128)S(1)}, f32[8,16,256]{2,1,0:T(8,128)}, f32[16,256]{1,0:T(8,128)S(1)}, f32[8,16,256]{2,1,0:T(8,128)S(1)}, /*index=5*/s32[]{:T(128)}, s32[]{:T(128)}) while((s32[]{:T(128)}, f32[16,256]{1,0:T(8,128)S(1)}, f32[8,16,256]{2,1,0:T(8,128)}, f32[16,256]{1,0:T(8,128)S(1)}, ...), condition=%wide.region_3.4_spmd.clone, body=%wide.region_2.3_spmd.clone.sunk | while | flops 16387 | bytes 98908 | solution.py:92
  198.6 35.4 %while.23 = (s32[]{:T(128)}, f32[16,256]{1,0:T(8,128)S(1)}, f32[16,256]{1,0:T(8,128)S(1)}, f32[16,256]{1,0:T(8,128)S(1)}, s32[]{:T(128)}) while((s32[]{:T(128)}, f32[16,256]{1,0:T(8,128)S(1)}, f32[16,256]{1,0:T(8,128)S(1)}, f32[16,256]{1,0:T(8,128)S(1)}, s32[]{:T(128)}) %tuple.55), condition=%wide.region_5.6_spmd, body=%wide.region_4.5_spmd.sunk | while | flops 8194 | bytes 131173 | solution.py:98
  198.6 1.9 collective-permute-start
  200.5 3.1 %collective-permute-done = f32[16,256]{1,0:T(8,128)S(1)} collective-permute-done((f32[16,256]{1,0:T(8,128)S(1)}, f32[16,256]{1,0:T(8,128)S(1)}, u32[]{:S(2)}, u32[]{:S(2)}) %collective-permute-start) | collective-permute-done | bytes 16416 | tf_op jit(solution)/shard_map/while/body/eval_jaxpr/ppermute | solution.py:12
  203.7 1.9 collective-permute-start
  205.6 3.1 %collective-permute-done = f32[16,256]{1,0:T(8,128)S(1)} collective-permute-done((f32[16,256]{1,0:T(8,128)S(1)}, f32[16,256]{1,0:T(8,128)S(1)}, u32[]{:S(2)}, u32[]{:S(2)}) %collective-permute-start) | collective-permute-done | bytes 16416 | tf_op jit(solution)/shard_map/while/body/eval_jaxpr/ppermute | solution.py:12
  208.7 1.9 collective-permute-start
  210.6 3.1 %collective-permute-done = f32[16,256]{1,0:T(8,128)S(1)} collective-permute-done((f32[16,256]{1,0:T(8,128)S(1)}, f32[16,256]{1,0:T(8,128)S(1)}, u32[]{:S(2)}, u32[]{:S(2)}) %collective-permute-start) | collective-permute-done | bytes 16416 | tf_op jit(solution)/shard_map/while/body/eval_jaxpr/ppermute | solution.py:12
  213.8 1.9 collective-permute-start
  215.7 3.1 %collective-permute-done = f32[16,256]{1,0:T(8,128)S(1)} collective-permute-done((f32[16,256]{1,0:T(8,128)S(1)}, f32[16,256]{1,0:T(8,128)S(1)}, u32[]{:S(2)}, u32[]{:S(2)}) %collective-permute-start) | collective-permute-done | bytes 16416 | tf_op jit(solution)/shard_map/while/body/eval_jaxpr/ppermute | solution.py:12
  218.8 1.9 collective-permute-start
  220.8 3.1 %collective-permute-done = f32[16,256]{1,0:T(8,128)S(1)} collective-permute-done((f32[16,256]{1,0:T(8,128)S(1)}, f32[16,256]{1,0:T(8,128)S(1)}, u32[]{:S(2)}, u32[]{:S(2)}) %collective-permute-start) | collective-permute-done | bytes 16416 | tf_op jit(solution)/shard_map/while/body/eval_jaxpr/ppermute | solution.py:12
  223.9 1.9 collective-permute-start
  225.8 3.1 %collective-permute-done = f32[16,256]{1,0:T(8,128)S(1)} collective-permute-done((f32[16,256]{1,0:T(8,128)S(1)}, f32[16,256]{1,0:T(8,128)S(1)}, u32[]{:S(2)}, u32[]{:S(2)}) %collective-permute-start) | collective-permute-done | bytes 16416 | tf_op jit(solution)/shard_map/while/body/eval_jaxpr/ppermute | solution.py:12
  228.9 1.9 collective-permute-start
  230.9 3.1 %collective-permute-done = f32[16,256]{1,0:T(8,128)S(1)} collective-permute-done((f32[16,256]{1,0:T(8,128)S(1)}, f32[16,256]{1,0:T(8,128)S(1)}, u32[]{:S(2)}, u32[]{:S(2)}) %collective-permute-start) | collective-permute-done | bytes 16416 | tf_op jit(solution)/shard_map/while/body/eval_jaxpr/ppermute | solution.py:12
  234.0 1.0 multiply_add_fusion.1
  235.0 1.3 copy.35
  236.3 37.7 %fusion.49 = f32[8,128,256]{1,0,2:T(8,128)S(1)} fusion(f32[8,128,256]{1,0,2:T(8,128)S(1)} %copy.29, f32[256,128,128]{2,0,1:T(8,128)} %fusion.2), kind=kOutput, calls=%fused_computation.59 | convolution fusion | flops 402653184 | bytes 18874368 | tf_op jit(solution)/shard_map/cts,jsc->jtc/dot_general | solution.py:81
  274.1 3.9 %fusion.52 = f32[8,128,256]{1,0,2:T(8,128)} fusion(f32[8,128,256]{1,0,2:T(8,128)S(1)} %fusion.49, f32[8,16,256]{1,0,2:T(8,128)S(1)} %copy-done, f32[128]{0:T(128)S(1)} %iota_add_fusion, f32[16,256]{0,1:T(8,128)S(1)} %copy-done.2, f32[16,256]{0,1:T(8,128)S(1)} %copy.28), kind=kOutput, calls=%fused_computation.60 | convolution fusion | flops 51642368 | bytes 2261504 | tf_op jit(solution)/shard_map/jmc,mtc->jtc/dot_general | solution.py:107
  277.9 1.6 copy.36
  279.9 24.5 %all_to_all.16 = bf16[32,32,256]{2,1,0:T(8,128)(2,1)S(1)} all-to-all(bf16[32,32,256]{2,1,0:T(8,128)(2,1)S(1)} %multiply_convert_fusion), channel_id=1, replica_groups=mesh['ctx'=8,'ch'=32] {'ch'}, dimensions={0} | all-to-all | bytes 1048576 | tf_op jit(solution)/shard_map/all_to_all | solution.py:110
  304.4 0.8 copy.45
  (73 shorter events, 7.5 us)
Async XLA Ops:
  6.5 43.5 %copy-start.4 = (f32[3,7,256]{2,1,0:T(8,128)S(1)}, f32[3,7,256]{2,1,0:T(8,128)}, u32[]{:S(2)}) copy-start(f32[3,7,256]{2,1,0:T(8,128)} %param.14) | copy-start | bytes 64516
  6.5 144.0 %all-gather.2.cloned.1.call-start = ((), (), s32[]{:S(2)}) async-start(), calls=%async_computation.1 | async-start | bytes 17301504 | tf_op jit(solution)/shard_map/all_gather | solution.py:19
  9.9 20.1 %collective-permute-start.2 = (bf16[3,1024,256]{2,1,0:T(8,128)(2,1)}, bf16[3,1024,256]{2,1,0:T(8,128)(2,1)S(1)}, u32[]{:S(2)}, u32[]{:S(2)}) collective-permute-start(bf16[3,1024,256]{2,1,0:T(8,128)(2,1)} %param.13), channel_id=1, source_target_pairs={{0,32},{32,64},{64,96},{96,128},{128,160},{160,192},{192,224},{224... | collective-permute-start | bytes 4718600 | tf_op jit(solution)/shard_map/ppermute | solution.py:39
  9.9 22.8 %collective-permute-start.1 = (bf16[3,1024,256]{2,1,0:T(8,128)(2,1)}, bf16[3,1024,256]{2,1,0:T(8,128)(2,1)}, u32[]{:S(2)}, u32[]{:S(2)}) collective-permute-start(bf16[3,1024,256]{2,1,0:T(8,128)(2,1)} %param.13), channel_id=1, source_target_pairs={{0,224},{32,0},{64,32},{96,64},{128,96},{160,128},{192,160},{224,1... | collective-permute-start | bytes 4718600 | tf_op jit(solution)/shard_map/ppermute | solution.py:41
  29.9 29.7 %copy-start.7 = (bf16[3,1024,256]{2,1,0:T(8,128)(2,1)}, bf16[3,1024,256]{2,1,0:T(8,128)(2,1)S(1)}, u32[]{:S(2)}) copy-start(bf16[3,1024,256]{2,1,0:T(8,128)(2,1)S(1)} %collective-permute-done.2) | copy-start | bytes 4718596
  29.9 19.9 %collective-permute-start.4 = (bf16[3,1024,256]{2,1,0:T(8,128)(2,1)S(1)}, bf16[3,1024,256]{2,1,0:T(8,128)(2,1)}, u32[]{:S(2)}, u32[]{:S(2)}) collective-permute-start(bf16[3,1024,256]{2,1,0:T(8,128)(2,1)S(1)} %collective-permute-done.2), channel_id=1, source_target_pairs={{0,32},{32,64},{64,96},{96,128},{128,160},{160,192},{192,224},{224... | collective-permute-start | bytes 4718600 | tf_op jit(solution)/shard_map/ppermute | solution.py:39
  32.7 27.0 %collective-permute-start.3 = (bf16[3,1024,256]{2,1,0:T(8,128)(2,1)}, bf16[3,1024,256]{2,1,0:T(8,128)(2,1)}, u32[]{:S(2)}, u32[]{:S(2)}) collective-permute-start(bf16[3,1024,256]{2,1,0:T(8,128)(2,1)} %collective-permute-done.1), channel_id=1, source_target_pairs={{0,224},{32,0},{64,32},{96,64},{128,96},{160,128},{192,160},{224,1... | collective-permute-start | bytes 4718600 | tf_op jit(solution)/shard_map/ppermute | solution.py:41
  49.9 20.2 %collective-permute-start.6 = (bf16[3,1024,256]{2,1,0:T(8,128)(2,1)}, bf16[3,1024,256]{2,1,0:T(8,128)(2,1)}, u32[]{:S(2)}, u32[]{:S(2)}) collective-permute-start(bf16[3,1024,256]{2,1,0:T(8,128)(2,1)} %collective-permute-done.4), channel_id=1, source_target_pairs={{0,32},{32,64},{64,96},{96,128},{128,160},{160,192},{192,224},{224... | collective-permute-start | bytes 4718600 | tf_op jit(solution)/shard_map/ppermute | solution.py:39
  59.7 109.8 %collective-permute-start.5 = (bf16[3,1024,256]{2,1,0:T(8,128)(2,1)}, bf16[3,1024,256]{2,1,0:T(8,128)(2,1)S(1)}, u32[]{:S(2)}, u32[]{:S(2)}) collective-permute-start(bf16[3,1024,256]{2,1,0:T(8,128)(2,1)} %collective-permute-done.3), channel_id=1, source_target_pairs={{0,224},{32,0},{64,32},{96,64},{128,96},{160,128},{192,160},{224,1... | collective-permute-start | bytes 4718600 | tf_op jit(solution)/shard_map/ppermute | solution.py:41
  70.0 102.9 %collective-permute-start.7 = (bf16[3,1024,256]{2,1,0:T(8,128)(2,1)}, bf16[3,1024,256]{2,1,0:T(8,128)(2,1)S(1)}, u32[]{:S(2)}, u32[]{:S(2)}) collective-permute-start(bf16[3,1024,256]{2,1,0:T(8,128)(2,1)} %collective-permute-done.6), channel_id=1, source_target_pairs={{0,32},{32,64},{64,96},{96,128},{128,160},{160,192},{192,224},{224... | collective-permute-start | bytes 4718600 | tf_op jit(solution)/shard_map/ppermute | solution.py:39
  150.5 8.6 %copy-start.1 = (bf16[1024,8192]{1,0:T(8,128)(2,1)S(1)}, bf16[1024,8192]{1,0:T(8,128)(2,1)}, u32[]{:S(2)}) copy-start(bf16[1024,8192]{1,0:T(8,128)(2,1)} %all-gather.2.cloned.1.call-done) | copy-start | bytes 50331652
  159.1 3.3 %copy-start.8 = (bf16[3,1024,256]{2,1,0:T(8,128)(2,1)S(1)}, bf16[3,1024,256]{2,1,0:T(8,128)(2,1)}, u32[]{:S(2)}) copy-start(bf16[3,1024,256]{2,1,0:T(8,128)(2,1)} %copy-done.7) | copy-start | bytes 4718596
  164.3 3.3 %copy-start.6 = (bf16[3,1024,256]{2,1,0:T(8,128)(2,1)S(1)}, bf16[3,1024,256]{2,1,0:T(8,128)(2,1)}, u32[]{:S(2)}) copy-start(bf16[3,1024,256]{2,1,0:T(8,128)(2,1)} %param.13) | copy-start | bytes 4718596
  172.9 7.2 %copy-start.3 = (f32[16,256]{1,0:T(8,128)S(1)}, f32[16,256]{1,0:T(8,128)}, u32[]{:S(2)}) copy-start(f32[16,256]{1,0:T(8,128)} %param.16) | copy-start | bytes 49156
  178.2 5.0 %collective-permute-start.8 = (bf16[3,6,256]{2,1,0:T(8,128)(2,1)S(1)}, bf16[3,6,256]{2,1,0:T(8,128)(2,1)S(1)}, u32[]{:S(2)}, u32[]{:S(2)}) collective-permute-start(bf16[3,6,256]{2,1,0:T(8,128)(2,1)S(1)} %slice.72), channel_id=1, source_target_pairs={{0,32},{32,64},{64,96},{96,128},{128,160},{160,192},{192,224},{1,3... | collective-permute-start | bytes 27656 | tf_op jit(solution)/shard_map/ppermute | solution.py:12
  198.6 5.1 %collective-permute-start = (f32[16,256]{1,0:T(8,128)S(1)}, f32[16,256]{1,0:T(8,128)S(1)}, u32[]{:S(2)}, u32[]{:S(2)}) collective-permute-start(f32[16,256]{1,0:T(8,128)S(1)} %multiply_add_fusion.3), channel_id=1, source_target_pairs={{0,32},{32,64},{64,96},{96,128},{128,160},{160,192},{192,224},{1,3... | collective-permute-start | bytes 49160 | tf_op jit(solution)/shard_map/while/body/eval_jaxpr/ppermute | solution.py:12
  203.7 5.0 %collective-permute-start = (f32[16,256]{1,0:T(8,128)S(1)}, f32[16,256]{1,0:T(8,128)S(1)}, u32[]{:S(2)}, u32[]{:S(2)}) collective-permute-start(f32[16,256]{1,0:T(8,128)S(1)} %multiply_add_fusion.3), channel_id=1, source_target_pairs={{0,32},{32,64},{64,96},{96,128},{128,160},{160,192},{192,224},{1,3... | collective-permute-start | bytes 49160 | tf_op jit(solution)/shard_map/while/body/eval_jaxpr/ppermute | solution.py:12
  208.7 5.0 %collective-permute-start = (f32[16,256]{1,0:T(8,128)S(1)}, f32[16,256]{1,0:T(8,128)S(1)}, u32[]{:S(2)}, u32[]{:S(2)}) collective-permute-start(f32[16,256]{1,0:T(8,128)S(1)} %multiply_add_fusion.3), channel_id=1, source_target_pairs={{0,32},{32,64},{64,96},{96,128},{128,160},{160,192},{192,224},{1,3... | collective-permute-start | bytes 49160 | tf_op jit(solution)/shard_map/while/body/eval_jaxpr/ppermute | solution.py:12
  213.8 5.0 %collective-permute-start = (f32[16,256]{1,0:T(8,128)S(1)}, f32[16,256]{1,0:T(8,128)S(1)}, u32[]{:S(2)}, u32[]{:S(2)}) collective-permute-start(f32[16,256]{1,0:T(8,128)S(1)} %multiply_add_fusion.3), channel_id=1, source_target_pairs={{0,32},{32,64},{64,96},{96,128},{128,160},{160,192},{192,224},{1,3... | collective-permute-start | bytes 49160 | tf_op jit(solution)/shard_map/while/body/eval_jaxpr/ppermute | solution.py:12
  218.8 5.0 %collective-permute-start = (f32[16,256]{1,0:T(8,128)S(1)}, f32[16,256]{1,0:T(8,128)S(1)}, u32[]{:S(2)}, u32[]{:S(2)}) collective-permute-start(f32[16,256]{1,0:T(8,128)S(1)} %multiply_add_fusion.3), channel_id=1, source_target_pairs={{0,32},{32,64},{64,96},{96,128},{128,160},{160,192},{192,224},{1,3... | collective-permute-start | bytes 49160 | tf_op jit(solution)/shard_map/while/body/eval_jaxpr/ppermute | solution.py:12
  223.9 5.0 %collective-permute-start = (f32[16,256]{1,0:T(8,128)S(1)}, f32[16,256]{1,0:T(8,128)S(1)}, u32[]{:S(2)}, u32[]{:S(2)}) collective-permute-start(f32[16,256]{1,0:T(8,128)S(1)} %multiply_add_fusion.3), channel_id=1, source_target_pairs={{0,32},{32,64},{64,96},{96,128},{128,160},{160,192},{192,224},{1,3... | collective-permute-start | bytes 49160 | tf_op jit(solution)/shard_map/while/body/eval_jaxpr/ppermute | solution.py:12
  228.9 5.0 %collective-permute-start = (f32[16,256]{1,0:T(8,128)S(1)}, f32[16,256]{1,0:T(8,128)S(1)}, u32[]{:S(2)}, u32[]{:S(2)}) collective-permute-start(f32[16,256]{1,0:T(8,128)S(1)} %multiply_add_fusion.3), channel_id=1, source_target_pairs={{0,32},{32,64},{64,96},{96,128},{128,160},{160,192},{192,224},{1,3... | collective-permute-start | bytes 49160 | tf_op jit(solution)/shard_map/while/body/eval_jaxpr/ppermute | solution.py:12
  236.3 37.7 %copy-start = (f32[8,16,256]{1,0,2:T(8,128)S(1)}, f32[8,16,256]{1,0,2:T(8,128)}, u32[]{:S(2)}) copy-start(f32[8,16,256]{1,0,2:T(8,128)} %copy.35) | copy-start | bytes 393220
  236.3 37.7 %copy-start.2 = (f32[16,256]{0,1:T(8,128)S(1)}, f32[16,256]{0,1:T(8,128)}, u32[]{:S(2)}) copy-start(f32[16,256]{0,1:T(8,128)} %copy.31) | copy-start | bytes 49156
  274.0 5.4 %copy-start.5 = (f32[256]{0:T(256)S(1)}, f32[256]{0:T(256)}, u32[]{:S(2)}) copy-start(f32[256]{0:T(256)} %param.17) | copy-start | bytes 3076
Sparse Core Ops, SparseCore 0:
  10.0 140.4 all-gather.1
